TPU v7x, 32 devices: a whole 2x2x4 slice. The times are simulated.
32 devices in a mesh: groups: 2 (over x), blk: 8 (over z, y), inner: 2 (over core).
Axes of the slice: x: 2, y: 2, z: 4, core: 2. Of those that a mesh axis runs over, the one named last changes fastest.
Arguments:
- patch_rows: bfloat16 [24576, 1536], P(('groups', 'blk', 'inner')), parts along dimension 0, may hold values from -6 to 6
- owner_ids: int32 [24576, 1], P(('groups', 'blk', 'inner')), parts along dimension 0, may hold values from 0 to 7; in each aligned block of 768 rows (0 to 767, 768 to 1535, ...) at most 192 rows name the same one
- page_ids: int32 [24576], P(('groups', 'blk', 'inner')), parts along dimension 0, may hold values from 0 to 7
- proj_weight: bfloat16 [1536, 128], replicated, may hold values from -0.15625 to 0.15625
- proj_bias: float32 [128], replicated, may hold values from -1.8 to 1.8
- query_tokens: bfloat16 [128, 32, 128], P(('groups', 'blk')), parts along dimension 0, may hold values from -0.5 to 0.5
- query_counts: int32 [128], P(('groups', 'blk')), parts along dimension 0, may hold values from 1 to 32, as said below
Outputs:
- page_scores: float32 [256, 64], P(('groups', 'blk', 'inner')), parts along dimension 0
There are 2 independent parts, one for each index of `groups`. A program takes and returns all parts, laid end to end along the dimension named above; an argument that names none is the same for every part. Nothing has to cross between parts.
Inputs may be any that keep to these rules, and one draw needn't show every extreme that they name: `owner_ids`: among the rows of one device, at most 192 name the same owner, a bound that some block reaches of them. `query_counts`: the first query of each part has all 32 tokens live.
All inputs are finite; a program needn't handle non-finite values.
Results may differ from a plain program's by a relative error of at most 0.00031.
Values may be sent and summed in bfloat16 or wider, within the bound.
No kernel may reach another device: no remote copies, remote signals or barrier semaphores. Data moves between devices by JAX's collectives and lax.ppermute only.
A program may use at most 64 MiB of HBM per device.

v0:
```python
import math
import jax
import jax.numpy as jnp
from jax import lax
from jax.sharding import PartitionSpec as P

PAGES_DEV = 8


def embed(rows, weight, bias):
    proj = jnp.dot(rows, weight, preferred_element_type=jnp.float32) + bias[None, :]
    scale = lax.rsqrt(jnp.sum(proj * proj, axis=1, keepdims=True) + 1e-06)
    return (proj * scale).astype(jnp.bfloat16)


def page_maxsim(tokens, counts, embedded, slot_pages, token_slots, page_total):
    sims = jnp.einsum("re,se->rs", tokens, embedded, preferred_element_type=jnp.float32)
    best = jnp.stack(
        [
            jnp.max(jnp.where(slot_pages[None, :] == page, sims, jnp.float32(-2.0)), axis=1)
            for page in range(page_total)
        ],
        axis=0,
    )
    best = best.reshape(page_total, counts.shape[0], token_slots)
    live = (jnp.arange(token_slots, dtype=jnp.int32)[None, :] < counts[:, None]).astype(jnp.float32)
    return jnp.sum(best * live[None, :, :], axis=2)


def make_scorer(embedded, slot_pages, page_total, token_slots, width):

    def score_block(carry, pieces, start):
        tokens, counts = pieces
        count_q = tokens.shape[0]
        group = math.gcd(count_q, max(1, 512 // token_slots))
        token_blocks = tokens.reshape(count_q // group, group * token_slots, width)
        count_blocks = counts.reshape(count_q // group, group)

        def one_block(args):
            block_tokens, block_counts = args
            return page_maxsim(
                block_tokens, block_counts, embedded, slot_pages, token_slots, page_total
            )

        scored = lax.map(one_block, (token_blocks, count_blocks))
        scored = jnp.transpose(scored, (1, 0, 2)).reshape(page_total, count_q)
        return scored

    return score_block


def shards(patch_rows, owner_ids, page_ids, proj_weight, proj_bias, query_tokens, query_counts):
    owners = lax.axis_size("blk")
    rows = patch_rows.shape[0]
    capacity = 2 * rows // owners
    slot_count = owners * capacity
    target = owner_ids[:, 0]
    onehot = (target[:, None] == jnp.arange(owners, dtype=jnp.int32)[None, :]).astype(jnp.int32)
    before = jnp.sum((jnp.cumsum(onehot, axis=0) - onehot) * onehot, axis=1)
    slot_index = target * capacity + before
    outgoing_pages = jnp.full((slot_count,), -1, jnp.int32).at[slot_index].set(page_ids)
    local = embed(patch_rows, proj_weight, proj_bias)
    packed = jnp.zeros((slot_count, local.shape[1]), jnp.bfloat16).at[slot_index].set(local)
    embedded, slot_pages = (
        lax.all_to_all(packed, "blk", split_axis=0, concat_axis=0, tiled=True),
        lax.all_to_all(outgoing_pages, "blk", split_axis=0, concat_axis=0, tiled=True),
    )
    per_block = query_tokens.shape[0]
    token_slots = query_tokens.shape[1]
    width = query_tokens.shape[2]
    total_queries = per_block * owners
    initial = jnp.zeros((PAGES_DEV, total_queries), jnp.float32)
    scorer = make_scorer(embedded, slot_pages, PAGES_DEV, token_slots, width)
    return scorer(
        initial,
        (
            lax.all_gather(query_tokens, "blk", axis=0, tiled=True),
            lax.all_gather(query_counts, "blk", axis=0, tiled=True),
        ),
        jnp.int32(0),
    )


def solution(mesh):
    in_specs = (
        P(("groups", "blk", "inner"), None),
        P(("groups", "blk", "inner"), None),
        P(("groups", "blk", "inner")),
        P(),
        P(),
        P(("groups", "blk"), None, None),
        P(("groups", "blk")),
    )
    out_specs = P(("groups", "blk", "inner"), None)
    return jax.shard_map(shards, mesh=mesh, in_specs=in_specs, out_specs=out_specs, check_vma=False)
```

profile of v0, /device:TPU:0, one launch (start us, length us, event | category | flops | bytes accessed | tf_op | source)
XLA Modules:
  0.0 88.6 jit_solution(12246551596819438382)
XLA Ops:
  0.0 0.8 reduce
  0.9 1.7 %reduce-window.6 = s32[8,6,128]{2,0,1:T(8,128)S(1)} reduce-window(s32[8,6,128]{2,0,1:T(8,128)S(1)} %fusion.10, s32[]{:T(128)} %copy.41), window={size=1x1x128 pad=0_0x0_0x127_0}, to_apply=%region_0.0 | reduce-window | flops 780288 | bytes 49156 | tf_op jit(solution)/shard_map/reduce-window
  2.7 0.1 copy.20
  2.8 0.2 reduce-window.9
  3.0 0.1 copy.21
  3.0 0.1 fusion.9
  3.1 0.7 fusion.13
  3.8 3.5 %scatter_custom_fusion = s32[1536]{0:T(1024)S(1)} fusion(s32[768]{0:T(1024)S(1)} %fusion.13, s32[768]{0:T(1024)} %param.11, s32[]{:T(128)} %constant.17.clone.1), kind=kCustom, calls=%fused_computation.49 | custom fusion | bytes 6656 | tf_op jit(solution)/shard_map/scatter | solution.py:61
  7.4 0.7 all_to_all.22
  8.1 7.3 %all-to-all-start = ((s32[8,192,1]{1,2,0:T(1,128)}), s32[8,192,1]{1,2,0:T(1,128)S(1)}, u32[]{:S(2)}, u32[]{:S(2)}) async-start(s32[8,192,1]{1,2,0:T(1,128)} %all_to_all.22), calls=%async_computation | async-start | bytes 16384 | tf_op jit(solution)/shard_map/all_to_all | solution.py:66
  15.4 1.9 %multiply_reduce_fusion.1 = (f32[768]{0:T(1024)S(1)}, f32[768,128]{0,1:T(8,128)S(1)}) fusion(f32[128]{0:T(128)} %param.13, bf16[768,1536]{1,0:T(8,128)(2,1)S(1)} %copy-done, bf16[1536,128]{1,0:T(8,128)(2,1)} %param.12), kind=kOutput, calls=%fused_computation.38 | convolution fusion | flops 302284032 | bytes 3149312 | tf_op jit(solution)/shard_map/dot_general | solution.py:11
  17.4 0.2 copy.23
  17.6 5.0 %scatter_custom_fusion.1 = bf16[1536,128]{1,0:T(8,128)(2,1)} fusion(s32[768]{0:T(1024)S(1)} %fusion.13, bf16[768,128]{1,0:T(8,128)(2,1)S(1)} %copy.23, bf16[]{:T(256)} %constant.13.clone.1), kind=kCustom, calls=%fused_computation.39 | custom fusion | bytes 393218 | tf_op jit(solution)/shard_map/scatter | solution.py:63
  22.6 6.0 %all-to-all-start.1 = ((bf16[8,192,128]{2,1,0:T(8,128)(2,1)}), bf16[8,192,128]{2,1,0:T(8,128)(2,1)S(1)}, u32[]{:S(2)}, u32[]{:S(2)}) async-start(bf16[8,192,128]{2,1,0:T(8,128)(2,1)} %bitcast.7), calls=%async_computation.1 | async-start | bytes 786432 | tf_op jit(solution)/shard_map/all_to_all | solution.py:65
  28.6 0.6 dynamic-slice
  29.9 0.2 dynamic-update-slice
  30.1 12.5 %all-reduce = s32[64]{0:T(128)S(1)} all-reduce(s32[64]{0:T(128)S(1)} %dynamic-update-slice), channel_id=1, replica_groups=mesh['groups'=2,'blk'=8,'inner'=2] {'blk'}, use_global_device_ids=true, to_apply=%add | all-reduce | flops 64 | bytes 512
  42.6 0.1 reshape.110
  42.7 31.5 %all_gather.6 = bf16[64,32,128]{2,1,0:T(8,128)(2,1)S(1)} all-gather(bf16[8,32,128]{2,1,0:T(8,128)(2,1)S(1)} %copy-done.1), channel_id=1, replica_groups=mesh['groups'=2,'blk'=8,'inner'=2] {'blk'}, dimensions={0}, use_global_device_ids=true | all-gather | bytes 589824 | tf_op jit(solution)/shard_map/all_gather | solution.py:77
  74.3 13.6 %while.10 = (s32[]{:T(128)}, f32[4,8,16]{2,1,0:T(8,128)S(1)}, s32[1536]{0:T(1024)S(1)}, bf16[4,512,128]{2,1,0:T(8,128)(2,1)S(1)}, bf16[1536,128]{1,0:T(8,128)(2,1)S(1)}, /*index=5*/s32[4,16]{1,0:T(4,128)S(1)}, s32[]{:T(128)}) while((s32[]{:T(128)}, f32[4,8,16]{2,1,0:T(8,128)S(1)}, s32[1536]{0:T(1024)S(1)}, ...), condition=%wide.region_16.17_spmd, body=%wide.region_6.16_spmd.sunk | while | flops 213926784 | bytes 762649 | solution.py:45
  74.3 2.5 %select_reduce_fusion.9 = (f32[512]{0:T(512)S(1)}, f32[512]{0:T(512)S(1)}, f32[512]{0:T(512)S(1)}, f32[512]{0:T(512)S(1)}, f32[512]{0:T(512)S(1)}, /*index=5*/f32[512]{0:T(512)S(1)}, f32[512]{0:T(512)S(1)}, f32[512]{0:T(512)S(1)}) fusion(pred[1536]{0:T(1024)(128)(4,1)S(1)} %get-tuple-element.121, pred[1536]{0:T(1024)(128)(4,1)S(1)} %get-tuple-element.122, ...), kind=kOutput, calls=%fused_computation.2.clone.1 | convolution fusion | flops 213905408 | bytes 557060 | tf_op jit(solution)/shard_map/while/body/eval_jaxpr/re,se->rs/dot_general | solution.py:17
  76.8 0.1 stack.35
  76.9 0.1 stack.36
  77.0 0.1 stack.37
  77.0 0.1 stack.38
  77.1 0.1 stack.39
  77.2 0.1 stack.40
  77.5 0.1 multiply_reduce_fusion.3
  77.7 2.5 %select_reduce_fusion.9 = (f32[512]{0:T(512)S(1)}, f32[512]{0:T(512)S(1)}, f32[512]{0:T(512)S(1)}, f32[512]{0:T(512)S(1)}, f32[512]{0:T(512)S(1)}, /*index=5*/f32[512]{0:T(512)S(1)}, f32[512]{0:T(512)S(1)}, f32[512]{0:T(512)S(1)}) fusion(pred[1536]{0:T(1024)(128)(4,1)S(1)} %get-tuple-element.121, pred[1536]{0:T(1024)(128)(4,1)S(1)} %get-tuple-element.122, ...), kind=kOutput, calls=%fused_computation.2.clone.1 | convolution fusion | flops 213905408 | bytes 557060 | tf_op jit(solution)/shard_map/while/body/eval_jaxpr/re,se->rs/dot_general | solution.py:17
  80.2 0.1 stack.35
  80.3 0.1 stack.36
  80.4 0.1 stack.37
  80.6 0.1 stack.40
  80.7 0.1 stack.41
  80.9 0.1 multiply_reduce_fusion.3
  81.1 2.5 %select_reduce_fusion.9 = (f32[512]{0:T(512)S(1)}, f32[512]{0:T(512)S(1)}, f32[512]{0:T(512)S(1)}, f32[512]{0:T(512)S(1)}, f32[512]{0:T(512)S(1)}, /*index=5*/f32[512]{0:T(512)S(1)}, f32[512]{0:T(512)S(1)}, f32[512]{0:T(512)S(1)}) fusion(pred[1536]{0:T(1024)(128)(4,1)S(1)} %get-tuple-element.121, pred[1536]{0:T(1024)(128)(4,1)S(1)} %get-tuple-element.122, ...), kind=kOutput, calls=%fused_computation.2.clone.1 | convolution fusion | flops 213905408 | bytes 557060 | tf_op jit(solution)/shard_map/while/body/eval_jaxpr/re,se->rs/dot_general | solution.py:17
  83.6 0.1 stack.35
  83.8 0.1 stack.38
  83.9 0.1 stack.39
  84.2 0.1 stack.42
  84.3 0.1 multiply_reduce_fusion.3
  84.5 2.5 %select_reduce_fusion.9 = (f32[512]{0:T(512)S(1)}, f32[512]{0:T(512)S(1)}, f32[512]{0:T(512)S(1)}, f32[512]{0:T(512)S(1)}, f32[512]{0:T(512)S(1)}, /*index=5*/f32[512]{0:T(512)S(1)}, f32[512]{0:T(512)S(1)}, f32[512]{0:T(512)S(1)}) fusion(pred[1536]{0:T(1024)(128)(4,1)S(1)} %get-tuple-element.121, pred[1536]{0:T(1024)(128)(4,1)S(1)} %get-tuple-element.122, ...), kind=kOutput, calls=%fused_computation.2.clone.1 | convolution fusion | flops 213905408 | bytes 557060 | tf_op jit(solution)/shard_map/while/body/eval_jaxpr/re,se->rs/dot_general | solution.py:17
  87.0 0.1 stack.35
  87.1 0.1 stack.36
  87.2 0.1 stack.37
  87.4 0.1 stack.40
  87.7 0.1 multiply_reduce_fusion.3
  87.9 0.7 reshape.111
  (80 shorter events, 1.8 us)
Async XLA Ops:
  0.0 15.4 %copy-start = (bf16[768,1536]{1,0:T(8,128)(2,1)S(1)}, bf16[768,1536]{1,0:T(8,128)(2,1)}, u32[]{:S(2)}) copy-start(bf16[768,1536]{1,0:T(8,128)(2,1)} %param.9) | copy-start | bytes 7077892
  8.1 14.5 %all-to-all-start = ((s32[8,192,1]{1,2,0:T(1,128)}), s32[8,192,1]{1,2,0:T(1,128)S(1)}, u32[]{:S(2)}, u32[]{:S(2)}) async-start(s32[8,192,1]{1,2,0:T(1,128)} %all_to_all.22), calls=%async_computation | async-start | bytes 16384 | tf_op jit(solution)/shard_map/all_to_all | solution.py:66
  15.4 13.2 %copy-start.3 = (u32[32]{0:T(128)S(1)}, u32[32]{0:T(128)}, u32[]{:S(2)}) copy-start(u32[32]{0:T(128)} %constant.55) | copy-start | bytes 388
  15.4 14.5 %copy-start.2 = (s32[8]{0:T(128)S(1)}, s32[8]{0:T(128)}, u32[]{:S(2)}) copy-start(s32[8]{0:T(128)} %param.15) | copy-start | bytes 100
  15.4 27.3 %copy-start.1 = (bf16[8,32,128]{2,1,0:T(8,128)(2,1)S(1)}, bf16[8,32,128]{2,1,0:T(8,128)(2,1)}, u32[]{:S(2)}) copy-start(bf16[8,32,128]{2,1,0:T(8,128)(2,1)} %param.14) | copy-start | bytes 196612
  22.6 51.7 %all-to-all-start.1 = ((bf16[8,192,128]{2,1,0:T(8,128)(2,1)}), bf16[8,192,128]{2,1,0:T(8,128)(2,1)S(1)}, u32[]{:S(2)}, u32[]{:S(2)}) async-start(bf16[8,192,128]{2,1,0:T(8,128)(2,1)} %bitcast.7), calls=%async_computation.1 | async-start | bytes 786432 | tf_op jit(solution)/shard_map/all_to_all | solution.py:65
where the time goes:
time: 88.9 us; the launch traced here: 88.6 us
  blocking collectives  44 us (49%)
  local copies, waits for them, and re-layouts  14.1 us (16%)
  starting transfers between devices  13.3 us (15%)
  matrix products  11.9 us (13%)
  other arithmetic  4.34 us (5%)
    all_gather x1, blocking collectives, shards(): lax.all_gather(query_tokens, 'blk', axis=0, tiled=True)  31.5 us
    unnamed x1, blocking collectives  12.5 us
    dot_general x4, matrix products, page_maxsim(): jnp.einsum('re,se->rs', tokens, embedded, preferred_element_type=jnp.floa...  9.97 us
    all_to_all x1, starting transfers between devices, shards(): lax.all_to_all(outgoing_pages, 'blk', split_axis=0, concat_axis=0, tiled=...  7.31 us
    all_to_all x1, starting transfers between devices, shards(): lax.all_to_all(packed, 'blk', split_axis=0, concat_axis=0, tiled=True)  5.99 us
    scatter x1, local copies, waits for them, and re-layouts, shards(): jnp.zeros((slot_count, local.shape[1]), jnp.bfloat16).at[slot_index]  4.98 us
    scatter x1, local copies, waits for them, and re-layouts, shards(): jnp.full((slot_count,), -1, jnp.int32).at[slot_index].set(page_ids)  3.54 us
    another operation x36, local copies, waits for them, and re-layouts, page_maxsim(): jnp.stack([jnp.max(jnp.where(slot_pages[None, :] == page, sims, jnp.float...  2.46 us
  transfers between devices with their start and end apart: 2, of which 0 were waited for; matrix products, arithmetic and copies ran while one was open for 9% of the time, Pallas kernels for 0%

commit v1 on v0

--- a/solution.py
+++ b/solution.py
@@ -5,6 +5,28 @@
 from jax.sharding import PartitionSpec as P
 
 PAGES_DEV = 8
+
+
+def in_blocks(x, dim, size):
+    before, after = (x.shape[:dim], x.shape[dim + 1 :])
+    return jnp.moveaxis(x.reshape(*before, size, -1, *after), dim, 0)
+
+
+def laid_out(tiles, dim):
+    tiles = jnp.moveaxis(tiles, 0, dim)
+    dims = tiles.shape
+    return tiles.reshape(*dims[:dim], dims[dim] * dims[dim + 1], *dims[dim + 2 :])
+
+
+def swapped_with_each(shard, axis, split_dim, concat_dim):
+    devices, index = (lax.axis_size(axis), lax.axis_index(axis))
+    pieces = in_blocks(shard, split_dim, devices)
+    outs = [pieces[index]]
+    for step in range(1, devices):
+        sent = pieces[index ^ step]
+        outs.append(lax.ppermute(sent, axis, [(i, i ^ step) for i in range(devices)]))
+    pieces = jnp.stack(outs)[index ^ jnp.arange(devices)]
+    return laid_out(pieces, concat_dim)
 
 
 def embed(rows, weight, bias):
@@ -62,7 +84,7 @@
     local = embed(patch_rows, proj_weight, proj_bias)
     packed = jnp.zeros((slot_count, local.shape[1]), jnp.bfloat16).at[slot_index].set(local)
     embedded, slot_pages = (
-        lax.all_to_all(packed, "blk", split_axis=0, concat_axis=0, tiled=True),
+        swapped_with_each(packed, "blk", 0, 0),
         lax.all_to_all(outgoing_pages, "blk", split_axis=0, concat_axis=0, tiled=True),
     )
     per_block = query_tokens.shape[0]

time: 88.9 us -> 107 us (1.20)
  local copies, waits for them, and re-layouts: 14.1 us -> 22.6 us
  starting transfers between devices: 13.3 us -> 19.1 us
  matrix products: 11.9 us -> 16.2 us
  blocking collectives: 44 us -> 42.8 us
    ppermute x0 -> x7, starting transfers between devices: none -> 14.2 us  [swapped_with_each(): lax.ppermute(sent, axis, [(i, i ^ step) for i in range(devices)])]
    all_to_all x1 -> x0, starting transfers between devices: 5.99 us -> none  [shards(): lax.all_to_all(packed, 'blk', split_axis=0, concat_axis=0, tiled=True)]
    dot_general x4, matrix products: 9.97 us -> 14.3 us  [page_maxsim(): jnp.einsum('re,se->rs', tokens, embedded, preferred_element_type=jnp.floa...]
    unnamed x11 -> x17, local copies, waits for them, and re-layouts: 0.92 us -> 4.99 us
    all_to_all x1, starting transfers between devices: 7.31 us -> 4.88 us  [shards(): lax.all_to_all(outgoing_pages, 'blk', split_axis=0, concat_axis=0, tiled=...]
    dynamic_update_slice x4, local copies, waits for them, and re-layouts: 0.03 us -> 2.39 us  [score_block(): scored = lax.map(one_block, (token_blocks, count_blocks))]
    unnamed x1, blocking collectives: 12.5 us -> 10.7 us
    gather x0 -> x1, local copies, waits for them, and re-layouts: none -> 1.33 us  [swapped_with_each(): pieces = jnp.stack(outs)[index ^ jnp.arange(devices)]]
  transfers between devices with their start and end apart: 2 -> 8, of which waited for: 0 -> 0; matrix products, arithmetic and copies ran while one was open for 9% -> 8% of each run, Pallas kernels for 0% -> 0%
where the time goes in v1:
time: 107 us; the launch traced here: 106 us
  blocking collectives  42.8 us (40%)
  local copies, waits for them, and re-layouts  22.6 us (21%)
  starting transfers between devices  19.1 us (18%)
  matrix products  16.2 us (15%)
  other arithmetic  4.34 us (4%)
    all_gather x1, blocking collectives, shards(): lax.all_gather(query_tokens, 'blk', axis=0, tiled=True)  32 us
    dot_general x4, matrix products, page_maxsim(): jnp.einsum('re,se->rs', tokens, embedded, preferred_element_type=jnp.floa...  14.3 us
    ppermute x7, starting transfers between devices, swapped_with_each(): lax.ppermute(sent, axis, [(i, i ^ step) for i in range(devices)])  14.2 us
    unnamed x1, blocking collectives  10.7 us
    unnamed x17, local copies, waits for them, and re-layouts  4.99 us
    all_to_all x1, starting transfers between devices, shards(): lax.all_to_all(outgoing_pages, 'blk', split_axis=0, concat_axis=0, tiled=...  4.88 us
    scatter x1, local copies, waits for them, and re-layouts, shards(): jnp.zeros((slot_count, local.shape[1]), jnp.bfloat16).at[slot_index]  4.36 us
    scatter x1, local copies, waits for them, and re-layouts, shards(): jnp.full((slot_count,), -1, jnp.int32).at[slot_index].set(page_ids)  3.54 us
  transfers between devices with their start and end apart: 8, of which 0 were waited for; matrix products, arithmetic and copies ran while one was open for 8% of the time, Pallas kernels for 0%

profile of v1, /device:TPU:0, one launch (start us, length us, event | category | flops | bytes accessed | tf_op | source)
XLA Modules:
  0.0 106.1 jit_solution(1863148095681323449)
XLA Ops:
  0.0 0.8 reduce
  0.9 1.7 %reduce-window.6 = s32[8,6,128]{2,0,1:T(8,128)S(1)} reduce-window(s32[8,6,128]{2,0,1:T(8,128)S(1)} %fusion.10, s32[]{:T(128)} %copy.48), window={size=1x1x128 pad=0_0x0_0x127_0}, to_apply=%region_0.0 | reduce-window | flops 780288 | bytes 49156 | tf_op jit(solution)/shard_map/reduce-window
  2.7 0.1 copy.20
  2.8 0.2 reduce-window.9
  3.0 0.1 copy.21
  3.0 0.1 fusion.9
  3.1 0.7 fusion.13
  3.9 1.9 %multiply_reduce_fusion.1 = (f32[768]{0:T(1024)S(1)}, f32[768,128]{0,1:T(8,128)S(1)}) fusion(f32[128]{0:T(128)} %param.13, bf16[768,1536]{1,0:T(8,128)(2,1)S(1)} %copy-done, bf16[1536,128]{1,0:T(8,128)(2,1)} %param.12), kind=kOutput, calls=%fused_computation.39 | convolution fusion | flops 302284032 | bytes 3149312 | tf_op jit(solution)/shard_map/dot_general | solution.py:33
  5.9 0.2 copy.23
  6.1 4.4 %scatter_custom_fusion.1 = bf16[1536,128]{1,0:T(8,128)(2,1)S(1)} fusion(s32[768]{0:T(1024)S(1)} %fusion.13, bf16[768,128]{1,0:T(8,128)(2,1)S(1)} %copy.23, bf16[]{:T(256)} %constant.13.clone.1), kind=kCustom, calls=%fused_computation.40 | custom fusion | bytes 393218 | tf_op jit(solution)/shard_map/scatter | solution.py:85
  10.5 0.7 dynamic-slice_bitcast_fusion
  11.1 3.0 %collective-permute-start = (bf16[192,128]{1,0:T(8,128)(2,1)}, bf16[192,128]{1,0:T(8,128)(2,1)}, u32[]{:S(2)}, u32[]{:S(2)}) collective-permute-start(bf16[192,128]{1,0:T(8,128)(2,1)} %get-tuple-element.72), channel_id=1, source_target_pairs={{0,2},{2,0},{4,6},{6,4},{8,10},{10,8},{12,14},{14,12},{1,3},{3,1},... | collective-permute-start | bytes 147464 | tf_op jit(solution)/shard_map/ppermute | solution.py:27
  14.1 1.6 %collective-permute-start.1 = (bf16[192,128]{1,0:T(8,128)(2,1)}, bf16[192,128]{1,0:T(8,128)(2,1)}, u32[]{:S(2)}, u32[]{:S(2)}) collective-permute-start(bf16[192,128]{1,0:T(8,128)(2,1)} %get-tuple-element.71), channel_id=1, source_target_pairs={{0,4},{2,6},{4,0},{6,2},{8,12},{10,14},{12,8},{14,10},{1,5},{3,7},... | collective-permute-start | bytes 147464 | tf_op jit(solution)/shard_map/ppermute | solution.py:27
  15.7 3.0 %collective-permute-start.3 = (bf16[192,128]{1,0:T(8,128)(2,1)S(1)}, bf16[192,128]{1,0:T(8,128)(2,1)}, u32[]{:S(2)}, u32[]{:S(2)}) collective-permute-start(bf16[192,128]{1,0:T(8,128)(2,1)S(1)} %get-tuple-element.69), channel_id=1, source_target_pairs={{0,8},{2,10},{4,12},{6,14},{8,0},{10,2},{12,4},{14,6},{1,9},{3,11}... | collective-permute-start | bytes 147464 | tf_op jit(solution)/shard_map/ppermute | solution.py:27
  18.7 1.3 %collective-permute-start.4 = (bf16[192,128]{1,0:T(8,128)(2,1)S(1)}, bf16[192,128]{1,0:T(8,128)(2,1)}, u32[]{:S(2)}, u32[]{:S(2)}) collective-permute-start(bf16[192,128]{1,0:T(8,128)(2,1)S(1)} %get-tuple-element.68), channel_id=1, source_target_pairs={{0,10},{2,8},{4,14},{6,12},{8,2},{10,0},{12,6},{14,4},{1,11},{3,9}... | collective-permute-start | bytes 147464 | tf_op jit(solution)/shard_map/ppermute | solution.py:27
  20.0 3.5 %scatter_custom_fusion = s32[1536]{0:T(1024)S(1)} fusion(s32[768]{0:T(1024)S(1)} %fusion.13, s32[768]{0:T(1024)} %param.11, s32[]{:T(128)} %constant.27.clone.1), kind=kCustom, calls=%fused_computation.66 | custom fusion | bytes 6656 | tf_op jit(solution)/shard_map/scatter | solution.py:83
  23.5 0.7 all_to_all.11
  24.2 4.9 %all-to-all-start = ((s32[8,192,1]{1,2,0:T(1,128)}), s32[8,192,1]{1,2,0:T(1,128)S(1)}, u32[]{:S(2)}, u32[]{:S(2)}) async-start(s32[8,192,1]{1,2,0:T(1,128)} %all_to_all.11), calls=%async_computation | async-start | bytes 16384 | tf_op jit(solution)/shard_map/all_to_all | solution.py:88
  29.1 32.0 %all_gather.6 = bf16[64,32,128]{2,1,0:T(8,128)(2,1)S(1)} all-gather(bf16[8,32,128]{2,1,0:T(8,128)(2,1)S(1)} %copy-done.1), channel_id=1, replica_groups=mesh['groups'=2,'blk'=8,'inner'=2] {'blk'}, dimensions={0}, use_global_device_ids=true | all-gather | bytes 589824 | tf_op jit(solution)/shard_map/all_gather | solution.py:99
  61.2 0.7 dynamic-slice
  62.6 0.2 dynamic-update-slice
  62.8 10.7 %all-reduce = s32[64]{0:T(128)S(1)} all-reduce(s32[64]{0:T(128)S(1)} %dynamic-update-slice), channel_id=1, replica_groups=mesh['groups'=2,'blk'=8,'inner'=2] {'blk'}, use_global_device_ids=true, to_apply=%add | all-reduce | flops 64 | bytes 512
  73.5 0.1 reshape.132
  73.7 1.1 %collective-permute-start.5 = (bf16[192,128]{1,0:T(8,128)(2,1)S(1)}, bf16[192,128]{1,0:T(8,128)(2,1)S(1)}, u32[]{:S(2)}, u32[]{:S(2)}) collective-permute-start(bf16[192,128]{1,0:T(8,128)(2,1)S(1)} %get-tuple-element.67), channel_id=1, source_target_pairs={{0,12},{2,14},{4,8},{6,10},{8,4},{10,6},{12,0},{14,2},{1,13},{3,15... | collective-permute-start | bytes 147464 | tf_op jit(solution)/shard_map/ppermute | solution.py:27
  74.8 0.8 bitcast_dynamic-update-slice_fusion.7
  75.7 4.2 %collective-permute-start.6 = (bf16[192,128]{1,0:T(8,128)(2,1)S(1)}, bf16[192,128]{1,0:T(8,128)(2,1)S(1)}, u32[]{:S(2)}, u32[]{:S(2)}) collective-permute-start(bf16[192,128]{1,0:T(8,128)(2,1)S(1)} %get-tuple-element.66), channel_id=1, source_target_pairs={{0,14},{2,12},{4,10},{6,8},{8,6},{10,4},{12,2},{14,0},{1,15},{3,13... | collective-permute-start | bytes 147464 | tf_op jit(solution)/shard_map/ppermute | solution.py:27
  79.9 0.8 bitcast_dynamic-update-slice_fusion.6
  80.7 0.8 bitcast_dynamic-update-slice_fusion.5
  81.5 0.8 bitcast_dynamic-update-slice_fusion.4
  82.3 0.8 bitcast_dynamic-update-slice_fusion.3
  83.2 1.3 %gather_fusion = bf16[8,192,128]{2,1,0:T(8,128)(2,1)} fusion(bf16[8,192,128]{2,1,0:T(8,128)(2,1)S(1)} %bitcast_dynamic-update-slice_fusion.1, s32[1024]{0:T(1024)S(1)} %pad_clamp_fusion), kind=kCustom, calls=%fused_computation | custom fusion | bytes 786464 | tf_op jit(solution)/shard_map/gather | solution.py:28
  84.5 20.2 %while.10 = (s32[]{:T(128)}, f32[4,8,16]{2,1,0:T(8,128)}, s32[1536]{0:T(1024)S(1)}, bf16[4,512,128]{2,1,0:T(8,128)(2,1)S(1)}, bf16[1536,128]{1,0:T(8,128)(2,1)}, /*index=5*/s32[4,16]{1,0:T(4,128)S(1)}, s32[]{:T(128)}) while((s32[]{:T(128)}, f32[4,8,16]{2,1,0:T(8,128)}, s32[1536]{0:T(1024)S(1)}, bf16[4,512,128]{2,1,0:T(8,128)(2,1)S(1)}, ...), condition=%wide.region_16.17_spmd, body=%wide.region_6.16_spmd.sunk | while | flops 213926784 | bytes 759573 | solution.py:67
  84.5 3.6 %select_reduce_fusion.9 = (f32[512]{0:T(512)S(1)}, f32[512]{0:T(512)S(1)}, f32[512]{0:T(512)S(1)}, f32[512]{0:T(512)S(1)}, f32[512]{0:T(512)S(1)}, /*index=5*/f32[512]{0:T(512)S(1)}, f32[512]{0:T(512)S(1)}, f32[512]{0:T(512)S(1)}) fusion(pred[1536]{0:T(1024)(128)(4,1)S(1)} %get-tuple-element.129, pred[1536]{0:T(1024)(128)(4,1)S(1)} %get-tuple-element.130, ...), kind=kOutput, calls=%fused_computation.3.clone.1 | convolution fusion | flops 213905408 | bytes 557060 | tf_op jit(solution)/shard_map/while/body/eval_jaxpr/re,se->rs/dot_general | solution.py:39
  88.8 0.1 multiply_reduce_fusion.3
  88.9 0.6 bitcast_dynamic-update-slice_fusion.9
  89.6 3.6 %select_reduce_fusion.9 = (f32[512]{0:T(512)S(1)}, f32[512]{0:T(512)S(1)}, f32[512]{0:T(512)S(1)}, f32[512]{0:T(512)S(1)}, f32[512]{0:T(512)S(1)}, /*index=5*/f32[512]{0:T(512)S(1)}, f32[512]{0:T(512)S(1)}, f32[512]{0:T(512)S(1)}) fusion(pred[1536]{0:T(1024)(128)(4,1)S(1)} %get-tuple-element.129, pred[1536]{0:T(1024)(128)(4,1)S(1)} %get-tuple-element.130, ...), kind=kOutput, calls=%fused_computation.3.clone.1 | convolution fusion | flops 213905408 | bytes 557060 | tf_op jit(solution)/shard_map/while/body/eval_jaxpr/re,se->rs/dot_general | solution.py:39
  93.1 0.1 stack.67
  93.9 0.1 multiply_reduce_fusion.3
  94.0 0.6 bitcast_dynamic-update-slice_fusion.9
  94.6 3.6 %select_reduce_fusion.9 = (f32[512]{0:T(512)S(1)}, f32[512]{0:T(512)S(1)}, f32[512]{0:T(512)S(1)}, f32[512]{0:T(512)S(1)}, f32[512]{0:T(512)S(1)}, /*index=5*/f32[512]{0:T(512)S(1)}, f32[512]{0:T(512)S(1)}, f32[512]{0:T(512)S(1)}) fusion(pred[1536]{0:T(1024)(128)(4,1)S(1)} %get-tuple-element.129, pred[1536]{0:T(1024)(128)(4,1)S(1)} %get-tuple-element.130, ...), kind=kOutput, calls=%fused_computation.3.clone.1 | convolution fusion | flops 213905408 | bytes 557060 | tf_op jit(solution)/shard_map/while/body/eval_jaxpr/re,se->rs/dot_general | solution.py:39
  98.9 0.1 multiply_reduce_fusion.3
  99.0 0.6 bitcast_dynamic-update-slice_fusion.9
  99.6 3.6 %select_reduce_fusion.9 = (f32[512]{0:T(512)S(1)}, f32[512]{0:T(512)S(1)}, f32[512]{0:T(512)S(1)}, f32[512]{0:T(512)S(1)}, f32[512]{0:T(512)S(1)}, /*index=5*/f32[512]{0:T(512)S(1)}, f32[512]{0:T(512)S(1)}, f32[512]{0:T(512)S(1)}) fusion(pred[1536]{0:T(1024)(128)(4,1)S(1)} %get-tuple-element.129, pred[1536]{0:T(1024)(128)(4,1)S(1)} %get-tuple-element.130, ...), kind=kOutput, calls=%fused_computation.3.clone.1 | convolution fusion | flops 213905408 | bytes 557060 | tf_op jit(solution)/shard_map/while/body/eval_jaxpr/re,se->rs/dot_general | solution.py:39
  103.2 0.1 stack.67
  104.0 0.1 multiply_reduce_fusion.3
  104.1 0.6 bitcast_dynamic-update-slice_fusion.9
  104.7 0.7 copy.24
  105.4 0.7 reshape.133
  (103 shorter events, 3.1 us)
Async XLA Ops:
  0.0 3.8 %copy-start = (bf16[768,1536]{1,0:T(8,128)(2,1)S(1)}, bf16[768,1536]{1,0:T(8,128)(2,1)}, u32[]{:S(2)}) copy-start(bf16[768,1536]{1,0:T(8,128)(2,1)} %param.9) | copy-start | bytes 7077892
  3.8 25.3 %copy-start.1 = (bf16[8,32,128]{2,1,0:T(8,128)(2,1)S(1)}, bf16[8,32,128]{2,1,0:T(8,128)(2,1)}, u32[]{:S(2)}) copy-start(bf16[8,32,128]{2,1,0:T(8,128)(2,1)} %param.14) | copy-start | bytes 196612
  3.9 57.3 %copy-start.3 = (u32[32]{0:T(128)S(1)}, u32[32]{0:T(128)}, u32[]{:S(2)}) copy-start(u32[32]{0:T(128)} %constant.79) | copy-start | bytes 388
  3.9 58.7 %copy-start.2 = (s32[8]{0:T(128)S(1)}, s32[8]{0:T(128)}, u32[]{:S(2)}) copy-start(s32[8]{0:T(128)} %param.15) | copy-start | bytes 100
  11.1 62.6 %collective-permute-start = (bf16[192,128]{1,0:T(8,128)(2,1)}, bf16[192,128]{1,0:T(8,128)(2,1)}, u32[]{:S(2)}, u32[]{:S(2)}) collective-permute-start(bf16[192,128]{1,0:T(8,128)(2,1)} %get-tuple-element.72), channel_id=1, source_target_pairs={{0,2},{2,0},{4,6},{6,4},{8,10},{10,8},{12,14},{14,12},{1,3},{3,1},... | collective-permute-start | bytes 147464 | tf_op jit(solution)/shard_map/ppermute | solution.py:27
  14.1 61.5 %collective-permute-start.1 = (bf16[192,128]{1,0:T(8,128)(2,1)}, bf16[192,128]{1,0:T(8,128)(2,1)}, u32[]{:S(2)}, u32[]{:S(2)}) collective-permute-start(bf16[192,128]{1,0:T(8,128)(2,1)} %get-tuple-element.71), channel_id=1, source_target_pairs={{0,4},{2,6},{4,0},{6,2},{8,12},{10,14},{12,8},{14,10},{1,5},{3,7},... | collective-permute-start | bytes 147464 | tf_op jit(solution)/shard_map/ppermute | solution.py:27
  15.7 65.0 %collective-permute-start.2 = (bf16[192,128]{1,0:T(8,128)(2,1)}, bf16[192,128]{1,0:T(8,128)(2,1)}, u32[]{:S(2)}, u32[]{:S(2)}) collective-permute-start(bf16[192,128]{1,0:T(8,128)(2,1)} %get-tuple-element.70), channel_id=1, source_target_pairs={{0,6},{2,4},{4,2},{6,0},{8,14},{10,12},{12,10},{14,8},{1,7},{3,5},... | collective-permute-start | bytes 147464 | tf_op jit(solution)/shard_map/ppermute | solution.py:27
  15.7 65.8 %collective-permute-start.3 = (bf16[192,128]{1,0:T(8,128)(2,1)S(1)}, bf16[192,128]{1,0:T(8,128)(2,1)}, u32[]{:S(2)}, u32[]{:S(2)}) collective-permute-start(bf16[192,128]{1,0:T(8,128)(2,1)S(1)} %get-tuple-element.69), channel_id=1, source_target_pairs={{0,8},{2,10},{4,12},{6,14},{8,0},{10,2},{12,4},{14,6},{1,9},{3,11}... | collective-permute-start | bytes 147464 | tf_op jit(solution)/shard_map/ppermute | solution.py:27
  18.7 63.6 %collective-permute-start.4 = (bf16[192,128]{1,0:T(8,128)(2,1)S(1)}, bf16[192,128]{1,0:T(8,128)(2,1)}, u32[]{:S(2)}, u32[]{:S(2)}) collective-permute-start(bf16[192,128]{1,0:T(8,128)(2,1)S(1)} %get-tuple-element.68), channel_id=1, source_target_pairs={{0,10},{2,8},{4,14},{6,12},{8,2},{10,0},{12,6},{14,4},{1,11},{3,9}... | collective-permute-start | bytes 147464 | tf_op jit(solution)/shard_map/ppermute | solution.py:27
  24.2 49.4 %all-to-all-start = ((s32[8,192,1]{1,2,0:T(1,128)}), s32[8,192,1]{1,2,0:T(1,128)S(1)}, u32[]{:S(2)}, u32[]{:S(2)}) async-start(s32[8,192,1]{1,2,0:T(1,128)} %all_to_all.11), calls=%async_computation | async-start | bytes 16384 | tf_op jit(solution)/shard_map/all_to_all | solution.py:88
  73.7 9.4 %collective-permute-start.5 = (bf16[192,128]{1,0:T(8,128)(2,1)S(1)}, bf16[192,128]{1,0:T(8,128)(2,1)S(1)}, u32[]{:S(2)}, u32[]{:S(2)}) collective-permute-start(bf16[192,128]{1,0:T(8,128)(2,1)S(1)} %get-tuple-element.67), channel_id=1, source_target_pairs={{0,12},{2,14},{4,8},{6,10},{8,4},{10,6},{12,0},{14,2},{1,13},{3,15... | collective-permute-start | bytes 147464 | tf_op jit(solution)/shard_map/ppermute | solution.py:27
  75.7 7.5 %collective-permute-start.6 = (bf16[192,128]{1,0:T(8,128)(2,1)S(1)}, bf16[192,128]{1,0:T(8,128)(2,1)S(1)}, u32[]{:S(2)}, u32[]{:S(2)}) collective-permute-start(bf16[192,128]{1,0:T(8,128)(2,1)S(1)} %get-tuple-element.66), channel_id=1, source_target_pairs={{0,14},{2,12},{4,10},{6,8},{8,6},{10,4},{12,2},{14,0},{1,15},{3,13... | collective-permute-start | bytes 147464 | tf_op jit(solution)/shard_map/ppermute | solution.py:27
